TPU v7x, 512 devices: a whole 4x4x16 slice. The times are simulated.
512 devices in a mesh: lon: 32 (over z, x_hi), lat: 16 (over x_lo, y, core).
Axes of the slice: x: 4 (x_hi: 2, x_lo: 2; x = x_hi * 2 + x_lo), y: 4, z: 16, core: 2. Of those that a mesh axis runs over, the one named last changes fastest.
Arguments:
- elevation: float32 [12, 1536, 4096], P(None, 'lat', 'lon'), may hold values from -6 to 6
- equilibrium: float32 [12, 1536, 4096], P(None, 'lat', 'lon'), may hold values from -4 to 4
- transport_u: float32 [12, 1536, 4096], P(None, 'lat', 'lon'), may hold values from -4 to 4
- transport_v: float32 [12, 1536, 4096], P(None, 'lat', 'lon'), may hold values from -4 to 4
- ocean_depth: float32 [1536, 4096], P('lat', 'lon'), may hold values from 0.3 to 3
- bottom_drag: float32 [1536, 4096], P('lat', 'lon'), may hold values from 0.2 to 2
- wet_mask: int32 [1536, 4096], P('lat', 'lon'), may hold values 0 or 1
- lon_green: float32 [4096, 128], P('lon'), may hold values from -0.5 to 0.5
- lat_green: float32 [1536, 49152], P('lat', 'lon'), may hold values from -0.0546875 to 0.0546875
Outputs:
- elevation_next: float32 [12, 1536, 4096], P(None, 'lat', 'lon')
- transport_u_next: float32 [12, 1536, 4096], P(None, 'lat', 'lon')
- transport_v_next: float32 [12, 1536, 4096], P(None, 'lat', 'lon')
All inputs are finite; a program needn't handle non-finite values. No bound on the sum of `wet_mask` on one device may be relied on, other than what follows from the above.
Results may differ from a plain program's by a relative error of at most 0.0001.
Values sent between devices are 32-bit elements; how exact they have to be, the bound alone decides.
No kernel may reach another device: no remote copies, remote signals or barrier semaphores. Data moves between devices by JAX's collectives and lax.ppermute only.
A program may use at most 64 MiB of HBM per device.

v0:
```python
import math
import jax
import jax.numpy as jnp
from jax import lax
from jax.sharding import PartitionSpec as P

FREQS = [1.9323, 2.0, 1.896, 2.0055, 1.0027, 0.9295]
VISCOSITY = 0.5


def extended(array, sides, width, wrap):
    for axis, dim in sides:
        size, length = (lax.axis_size(axis), array.shape[dim])
        up = [(i, (i + 1) % size) for i in range(size if wrap else size - 1)]
        down = [(j, i) for i, j in up]
        last = lax.slice_in_dim(array, length - width, length, axis=dim)
        initial = lax.slice_in_dim(array, 0, width, axis=dim)
        before = lax.ppermute(last, axis, up)
        after = lax.ppermute(initial, axis, down)
        array = jnp.concatenate([before, array, after], axis=dim)
    return array


def row_terms(rows, nlat):
    angle = (-80.0 + 160.0 * (rows.astype(jnp.float32) + 0.5) / nlat) * (math.pi / 180.0)
    return ((1.0 / jnp.cos(angle))[:, None], (2.0 * jnp.sin(angle))[:, None])


def extend(stack, width):
    widened = extended(stack, (("lon", 2),), width, True)
    return extended(widened, (("lat", 1),), width, False)


def slopes(potential_ext, stretch):
    east_slope = (potential_ext[:, 1:-1, 2:] - potential_ext[:, 1:-1, :-2]) * 0.5 * stretch
    north_slope = (potential_ext[:, 2:, 1:-1] - potential_ext[:, :-2, 1:-1]) * 0.5
    return (east_slope, north_slope)


def solve_cells(push_u, push_v, drag_field, wet_frac, coriolis):
    damping = drag_field + 4.0 * VISCOSITY
    frequency = jnp.array(FREQS, jnp.float32)[:, None, None]
    det_real = damping * damping - frequency * frequency + coriolis * coriolis
    det_imag = 2.0 * damping * frequency
    magnitude = det_real * det_real + det_imag * det_imag

    def combine(first, second, factor):
        top_real = damping * first[:6] - frequency * first[6:] + factor * coriolis * second[:6]
        top_imag = damping * first[6:] + frequency * first[:6] + factor * coriolis * second[6:]
        out_real = (top_real * det_real + top_imag * det_imag) / magnitude
        out_imag = (top_imag * det_real - top_real * det_imag) / magnitude
        return wet_frac * jnp.concatenate([out_real, out_imag], axis=0)

    return jnp.concatenate([combine(push_u, push_v, 1.0), combine(push_v, push_u, -1.0)], axis=0)


def relax(flow_ext, east_slope, north_slope, depth_field, drag_field, wet_frac, coriolis):
    beside_all = (
        flow_ext[:, :-2, 1:-1]
        + flow_ext[:, 2:, 1:-1]
        + flow_ext[:, 1:-1, :-2]
        + flow_ext[:, 1:-1, 2:]
    )
    push_u = -depth_field * east_slope + VISCOSITY * beside_all[:12]
    push_v = -depth_field * north_slope + VISCOSITY * beside_all[12:]
    return solve_cells(push_u, push_v, drag_field, wet_frac, coriolis)


def surface(east_ext, north_ext, stretch, wet_frac):
    spread = (east_ext[:, :, 2:] - east_ext[:, :, :-2]) * 0.5 * stretch + (
        north_ext[:, 2:, :] - north_ext[:, :-2, :]
    ) * 0.5
    frequency = jnp.array(FREQS, jnp.float32)[:, None, None]
    return wet_frac * jnp.concatenate([-spread[6:] / frequency, spread[:6] / frequency], axis=0)


def per_device(
    elevation,
    equilibrium,
    transport_u,
    transport_v,
    ocean_depth,
    bottom_drag,
    wet_mask,
    lon_green,
    lat_green,
):
    rows_here = elevation.shape[1]
    total_rows = rows_here * lax.axis_size("lat")
    wet_frac = wet_mask.astype(jnp.float32)
    source = wet_frac * elevation
    mixed = jnp.einsum("krj,cj->krc", source, lon_green, precision=lax.Precision.HIGHEST)
    sal = jnp.einsum(
        "rs,ksc->krc",
        lat_green,
        lax.all_gather(mixed, "lat", axis=1, tiled=True),
        precision=lax.Precision.HIGHEST,
    )
    potential = elevation - equilibrium - sal
    first_row = lax.axis_index("lat") * rows_here
    stretch, coriolis = row_terms(first_row + jnp.arange(rows_here), total_rows)
    flows = jnp.concatenate([transport_u, transport_v], axis=0)
    widened = extend(jnp.concatenate([potential, flows], axis=0), 1)
    east_slope, north_slope = slopes(widened[:12], stretch)
    flows = relax(
        widened[12:], east_slope, north_slope, ocean_depth, bottom_drag, wet_frac, coriolis
    )
    flows = relax(
        extend(flows, 1), east_slope, north_slope, ocean_depth, bottom_drag, wet_frac, coriolis
    )
    around_all = extend(flows, 1)
    east_ext = around_all[:12, 1:-1, :]
    north_ext = around_all[12:, :, 1:-1]
    elevation_next = surface(east_ext, north_ext, stretch, wet_frac)
    return (elevation_next, flows[:12], flows[12:])


def solution(mesh):
    placed = (
        P(None, "lat", "lon"),
        P(None, "lat", "lon"),
        P(None, "lat", "lon"),
        P(None, "lat", "lon"),
        P("lat", "lon"),
        P("lat", "lon"),
        P("lat", "lon"),
        P("lon", None),
        P("lat", "lon"),
    )
    return jax.shard_map(
        per_device,
        mesh=mesh,
        in_specs=placed,
        out_specs=(P(None, "lat", "lon"), P(None, "lat", "lon"), P(None, "lat", "lon")),
        check_vma=False,
    )
```

profile of v0, /device:TPU:2, one launch (start us, length us, event | category | flops | bytes accessed | tf_op | source)
XLA Modules:
  0.0 202.3 jit_solution(10215366285293022981)
XLA Ops:
  8.8 2.5 %fusion.20 = f32[12,96,128]{2,1,0:T(8,128)} fusion(f32[12,96,128]{2,1,0:T(8,128)} %param.12, f32[96,128]{1,0:T(8,128)S(1)} %convert_element_type.21, f32[128,128]{1,0:T(8,128)} %param.19), kind=kOutput, calls=%fused_computation.86 | convolution fusion | flops 226639872 | bytes 1294336 | tf_op jit(solution)/shard_map/krj,cj->krc/dot_general | solution.py:92
  13.3 67.3 %all-gather.2.cloned.1.call-done = f32[12,1536,128]{2,1,0:T(8,128)} async-done(((f32[12,96,128]{2,1,0:T(8,128)}), f32[12,1536,128]{2,1,0:T(8,128)}) %all-gather.2.cloned.1.call-update) | async-done | bytes 9437200 | tf_op jit(solution)/shard_map/all_gather | solution.py:96
  80.6 8.3 %fusion = f32[12,96,128]{2,1,0:T(8,128)S(1)} fusion(f32[12,1536,128]{2,1,0:T(8,128)} %all-gather.2.cloned.1.call-done, f32[96,1536]{1,0:T(8,128)S(1)} %copy-done, f32[12,96,128]{2,1,0:T(8,128)S(1)} %copy-done.11, f32[12,96,128]{2,1,0:T(8,128)S(1)} %copy-done.21), kind=kOutput, calls=%fused_computation.11 | convolution fusion | flops 2718203904 | bytes 11796480 | tf_op jit(solution)/shard_map/rs,ksc->krc/dot_general | solution.py:93
  89.1 1.9 fusion.56
  91.0 2.6 %copy.15 = f32[36,96,1]{1,2,0:T(1,128)} copy(f32[36,96,1]{2,1,0:T(8,128)} %get-tuple-element.26) | data formatting | bytes 27648 | tf_op jit(solution)/shard_map/slice | solution.py:17
  93.6 7.5 %collective-permute-start = (f32[36,96,1]{1,2,0:T(1,128)}, f32[36,96,1]{1,2,0:T(1,128)}, u32[]{:S(2)}, u32[]{:S(2)}) collective-permute-start(f32[36,96,1]{1,2,0:T(1,128)} %copy.15), channel_id=1, source_target_pairs={{16,0},{32,16},{48,32},{64,48},{80,64},{96,80},{112,96},{128,112},... | collective-permute-start | bytes 41480 | tf_op jit(solution)/shard_map/ppermute | solution.py:19
  101.0 1.1 copy.17
  102.2 1.9 collective-permute-start.1
  104.2 1.3 copy.16
  105.5 6.3 %collective-permute-done.1 = f32[36,96,1]{1,2,0:T(1,128)} collective-permute-done((f32[36,96,1]{1,2,0:T(1,128)}, f32[36,96,1]{1,2,0:T(1,128)}, u32[]{:S(2)}, u32[]{:S(2)}) %collective-permute-start.1) | collective-permute-done | bytes 13856 | tf_op jit(solution)/shard_map/ppermute | solution.py:18
  111.8 2.5 %copy.18 = f32[36,96,1]{2,1,0:T(8,128)} copy(f32[36,96,1]{1,2,0:T(1,128)} %collective-permute-done.1) | data formatting | bytes 27648 | tf_op jit(solution)/shard_map/ppermute | solution.py:18
  114.3 1.4 pad_maximum_fusion.47
  115.7 1.9 collective-permute-start.2
  117.7 5.8 %collective-permute-start.3 = (f32[36,1,130]{2,1,0:T(1,128)S(1)}, f32[36,1,130]{2,1,0:T(1,128)S(1)}, u32[]{:S(2)}, u32[]{:S(2)}) collective-permute-start(f32[36,1,130]{2,1,0:T(1,128)S(1)} %get-tuple-element.20), channel_id=1, source_target_pairs={{1,0},{2,1},{3,2},{4,3},{5,4},{6,5},{7,6},{8,7},{9,8},{10,9},{11,1... | collective-permute-start | bytes 56168 | tf_op jit(solution)/shard_map/ppermute | solution.py:19
  123.5 1.5 collective-permute-done.3
  125.0 2.3 %fusion.4 = f32[24,96,128]{2,1,0:T(8,128)S(1)} fusion(f32[36,96,1]{2,1,0:T(8,128)S(1)} %copy.16, f32[12,96,128]{2,1,0:T(8,128)S(1)} %copy-done.2, f32[12,96,128]{2,1,0:T(8,128)S(1)} %copy-done.4, f32[12,96,128]{2,1,0:T(8,128)S(1)} %fusion, f32[36,96,1]{2,1,0:T(8,128)S(1)} %copy-done.1, f32[36,1,130]{2,1,0:T(1,128)S(1)} %collective-permute-done.3, ...), kind=kLoop, calls=%fused_computation.32 | loop fusion | flops 5603328 | bytes 3014208 | tf_op jit(solution)/shard_map/add | solution.py:59
  127.4 1.4 fusion.16
  128.8 1.3 fusion.13
  132.8 1.9 collective-permute-start.4
  135.1 7.5 %collective-permute-start.5 = (f32[24,96,1]{1,0,2:T(8,128)S(1)}, f32[24,96,1]{1,0,2:T(8,128)}, u32[]{:S(2)}, u32[]{:S(2)}) collective-permute-start(f32[24,96,1]{1,0,2:T(8,128)S(1)} %copy.22), channel_id=1, source_target_pairs={{16,0},{32,16},{48,32},{64,48},{80,64},{96,80},{112,96},{128,112},... | collective-permute-start | bytes 27656 | tf_op jit(solution)/shard_map/ppermute | solution.py:19
  144.0 1.1 copy.24
  146.3 1.9 collective-permute-start.6
  148.2 6.1 %collective-permute-start.7 = (f32[24,1,130]{2,1,0:T(1,128)S(1)}, f32[24,1,130]{2,1,0:T(1,128)S(1)}, u32[]{:S(2)}, u32[]{:S(2)}) collective-permute-start(f32[24,1,130]{2,1,0:T(1,128)S(1)} %get-tuple-element.24), channel_id=1, source_target_pairs={{1,0},{2,1},{3,2},{4,3},{5,4},{6,5},{7,6},{8,7},{9,8},{10,9},{11,1... | collective-permute-start | bytes 37448 | tf_op jit(solution)/shard_map/ppermute | solution.py:19
  154.3 1.3 collective-permute-done.7
  155.6 1.6 fusion.1
  160.8 7.9 %collective-permute-start.8 = (f32[24,96,1]{1,0,2:T(8,128)S(1)}, f32[24,96,1]{1,0,2:T(8,128)S(1)}, u32[]{:S(2)}, u32[]{:S(2)}) collective-permute-start(f32[24,96,1]{1,0,2:T(8,128)S(1)} %copy.27), channel_id=1, source_target_pairs={{16,0},{32,16},{48,32},{64,48},{80,64},{96,80},{112,96},{128,112},... | collective-permute-start | bytes 27656 | tf_op jit(solution)/shard_map/ppermute | solution.py:19
  169.1 1.9 collective-permute-start.9
  171.5 6.9 %collective-permute-done.9 = f32[24,96,1]{1,0,2:T(8,128)} collective-permute-done((f32[24,96,1]{1,0,2:T(8,128)S(1)}, f32[24,96,1]{1,0,2:T(8,128)}, u32[]{:S(2)}, u32[]{:S(2)}) %collective-permute-start.9) | collective-permute-done | bytes 9248 | tf_op jit(solution)/shard_map/ppermute | solution.py:18
  178.4 1.1 copy.30
  180.7 4.9 %collective-permute-start.10 = (f32[24,1,130]{2,1,0:T(1,128)S(1)}, f32[24,1,130]{2,1,0:T(1,128)S(1)}, u32[]{:S(2)}, u32[]{:S(2)}) collective-permute-start(f32[24,1,130]{2,1,0:T(1,128)S(1)} %get-tuple-element.21), channel_id=1, source_target_pairs={{1,0},{2,1},{3,2},{4,3},{5,4},{6,5},{7,6},{8,7},{9,8},{10,9},{11,1... | collective-permute-start | bytes 37448 | tf_op jit(solution)/shard_map/ppermute | solution.py:19
  185.6 1.9 collective-permute-start.11
  187.5 5.3 %collective-permute-done.11 = f32[24,1,130]{2,1,0:T(1,128)S(1)} collective-permute-done((f32[24,1,130]{2,1,0:T(1,128)S(1)}, f32[24,1,130]{2,1,0:T(1,128)S(1)}, u32[]{:S(2)}, u32[]{:S(2)}) %collective-permute-start.11) | collective-permute-done | bytes 12512 | tf_op jit(solution)/shard_map/ppermute | solution.py:18
  (116 shorter events, 17.1 us)
Async XLA Ops:
  7.2 73.4 %copy-start = (f32[96,1536]{1,0:T(8,128)S(1)}, f32[96,1536]{1,0:T(8,128)}, u32[]{:S(2)}) copy-start(f32[96,1536]{1,0:T(8,128)} %param.20) | copy-start | bytes 1769476
  7.2 73.4 %copy-start.11 = (f32[12,96,128]{2,1,0:T(8,128)S(1)}, f32[12,96,128]{2,1,0:T(8,128)}, u32[]{:S(2)}) copy-start(f32[12,96,128]{2,1,0:T(8,128)} %param.12) | copy-start | bytes 1769476
  7.2 4.8 %copy-start.26 = (f32[96,128]{1,0:T(8,128)S(1)}, f32[96,128]{1,0:T(8,128)}, u32[]{:S(2)}) copy-start(f32[96,128]{1,0:T(8,128)} %param.16) | copy-start | bytes 147460
  7.2 5.4 %copy-start.27 = (f32[96,128]{1,0:T(8,128)S(1)}, f32[96,128]{1,0:T(8,128)}, u32[]{:S(2)}) copy-start(f32[96,128]{1,0:T(8,128)} %param.17) | copy-start | bytes 147460
  7.2 73.4 %copy-start.21 = (f32[12,96,128]{2,1,0:T(8,128)S(1)}, f32[12,96,128]{2,1,0:T(8,128)}, u32[]{:S(2)}) copy-start(f32[12,96,128]{2,1,0:T(8,128)} %param.13) | copy-start | bytes 1769476
  7.2 73.4 %all-gather.2.cloned.1.call-start = ((), (), s32[]{:S(2)}) async-start(), calls=%async_computation | async-start | bytes 10027008 | tf_op jit(solution)/shard_map/all_gather | solution.py:96
  12.0 118.2 %copy-start.35 = (f32[96]{0:T(128)}, f32[96]{0:T(128)S(1)}, u32[]{:S(2)}) copy-start(f32[96]{0:T(128)S(1)} %get-tuple-element.54) | copy-start | bytes 1156
  13.3 75.6 %copy-start.2 = (f32[12,96,128]{2,1,0:T(8,128)S(1)}, f32[12,96,128]{2,1,0:T(8,128)}, u32[]{:S(2)}) copy-start(f32[12,96,128]{2,1,0:T(8,128)} %param.15) | copy-start | bytes 1769476
  13.3 75.6 %copy-start.3 = (f32[12,96,128]{2,1,0:T(8,128)S(1)}, f32[12,96,128]{2,1,0:T(8,128)}, u32[]{:S(2)}) copy-start(f32[12,96,128]{2,1,0:T(8,128)} %param.14) | copy-start | bytes 1769476
  93.6 10.6 %collective-permute-start = (f32[36,96,1]{1,2,0:T(1,128)}, f32[36,96,1]{1,2,0:T(1,128)}, u32[]{:S(2)}, u32[]{:S(2)}) collective-permute-start(f32[36,96,1]{1,2,0:T(1,128)} %copy.15), channel_id=1, source_target_pairs={{16,0},{32,16},{48,32},{64,48},{80,64},{96,80},{112,96},{128,112},... | collective-permute-start | bytes 41480 | tf_op jit(solution)/shard_map/ppermute | solution.py:19
  102.2 9.6 %collective-permute-start.1 = (f32[36,96,1]{1,2,0:T(1,128)}, f32[36,96,1]{1,2,0:T(1,128)}, u32[]{:S(2)}, u32[]{:S(2)}) collective-permute-start(f32[36,96,1]{1,2,0:T(1,128)} %copy.17), channel_id=1, source_target_pairs={{0,16},{16,32},{32,48},{48,64},{64,80},{80,96},{96,112},{112,128},... | collective-permute-start | bytes 41480 | tf_op jit(solution)/shard_map/ppermute | solution.py:18
  104.2 23.2 %copy-start.33 = (f32[96]{0:T(128)}, f32[96]{0:T(128)S(1)}, u32[]{:S(2)}) copy-start(f32[96]{0:T(128)S(1)} %divide_multiply_fusion) | copy-start | bytes 1156
  114.3 10.7 %copy-start.1 = (f32[36,96,1]{2,1,0:T(8,128)S(1)}, f32[36,96,1]{2,1,0:T(8,128)}, u32[]{:S(2)}) copy-start(f32[36,96,1]{2,1,0:T(8,128)} %copy.18) | copy-start | bytes 41476
  114.3 10.7 %copy-start.4 = (f32[12,96,128]{2,1,0:T(8,128)S(1)}, f32[12,96,128]{2,1,0:T(8,128)}, u32[]{:S(2)}) copy-start(f32[12,96,128]{2,1,0:T(8,128)} %param.14) | copy-start | bytes 1769476
  115.7 7.8 %collective-permute-start.2 = (f32[36,1,130]{2,1,0:T(1,128)S(1)}, f32[36,1,130]{2,1,0:T(1,128)S(1)}, u32[]{:S(2)}, u32[]{:S(2)}) collective-permute-start(f32[36,1,130]{2,1,0:T(1,128)S(1)} %get-tuple-element.19), channel_id=1, source_target_pairs={{0,1},{1,2},{2,3},{3,4},{4,5},{5,6},{6,7},{7,8},{8,9},{9,10},{10,1... | collective-permute-start | bytes 56168 | tf_op jit(solution)/shard_map/ppermute | solution.py:18
  117.7 7.4 %collective-permute-start.3 = (f32[36,1,130]{2,1,0:T(1,128)S(1)}, f32[36,1,130]{2,1,0:T(1,128)S(1)}, u32[]{:S(2)}, u32[]{:S(2)}) collective-permute-start(f32[36,1,130]{2,1,0:T(1,128)S(1)} %get-tuple-element.20), channel_id=1, source_target_pairs={{1,0},{2,1},{3,2},{4,3},{5,4},{6,5},{7,6},{8,7},{9,8},{10,9},{11,1... | collective-permute-start | bytes 56168 | tf_op jit(solution)/shard_map/ppermute | solution.py:19
  123.5 7.3 %copy-start.31 = (f32[96]{0:T(128)}, f32[96]{0:T(128)S(1)}, u32[]{:S(2)}) copy-start(f32[96]{0:T(128)S(1)} %fusion.52) | copy-start | bytes 1156
  132.8 9.9 %collective-permute-start.4 = (f32[24,96,1]{1,0,2:T(8,128)S(1)}, f32[24,96,1]{1,0,2:T(8,128)S(1)}, u32[]{:S(2)}, u32[]{:S(2)}) collective-permute-start(f32[24,96,1]{1,0,2:T(8,128)S(1)} %copy.21), channel_id=1, source_target_pairs={{0,16},{16,32},{32,48},{48,64},{64,80},{80,96},{96,112},{112,128},... | collective-permute-start | bytes 27656 | tf_op jit(solution)/shard_map/ppermute | solution.py:18
  135.1 8.9 %collective-permute-start.5 = (f32[24,96,1]{1,0,2:T(8,128)S(1)}, f32[24,96,1]{1,0,2:T(8,128)}, u32[]{:S(2)}, u32[]{:S(2)}) collective-permute-start(f32[24,96,1]{1,0,2:T(8,128)S(1)} %copy.22), channel_id=1, source_target_pairs={{16,0},{32,16},{48,32},{64,48},{80,64},{96,80},{112,96},{128,112},... | collective-permute-start | bytes 27656 | tf_op jit(solution)/shard_map/ppermute | solution.py:19
  145.2 10.5 %copy-start.9 = (f32[12,96,128]{2,1,0:T(8,128)S(1)}, f32[12,96,128]{2,1,0:T(8,128)}, u32[]{:S(2)}) copy-start(f32[12,96,128]{2,1,0:T(8,128)} %copy-done.8) | copy-start | bytes 1769476
  146.3 8.0 %collective-permute-start.6 = (f32[24,1,130]{2,1,0:T(1,128)S(1)}, f32[24,1,130]{2,1,0:T(1,128)S(1)}, u32[]{:S(2)}, u32[]{:S(2)}) collective-permute-start(f32[24,1,130]{2,1,0:T(1,128)S(1)} %get-tuple-element.23), channel_id=1, source_target_pairs={{0,1},{1,2},{2,3},{3,4},{4,5},{5,6},{6,7},{7,8},{8,9},{9,10},{10,1... | collective-permute-start | bytes 37448 | tf_op jit(solution)/shard_map/ppermute | solution.py:18
  148.2 9.1 %copy-start.10 = (f32[12,96,128]{2,1,0:T(8,128)S(1)}, f32[12,96,128]{2,1,0:T(8,128)}, u32[]{:S(2)}) copy-start(f32[12,96,128]{2,1,0:T(8,128)} %get-tuple-element.16) | copy-start | bytes 1769476
  148.2 9.1 %copy-start.12 = (f32[12,96,128]{2,1,0:T(8,128)S(1)}, f32[12,96,128]{2,1,0:T(8,128)}, u32[]{:S(2)}) copy-start(f32[12,96,128]{2,1,0:T(8,128)} %get-tuple-element.18) | copy-start | bytes 1769476
  148.2 7.4 %collective-permute-start.7 = (f32[24,1,130]{2,1,0:T(1,128)S(1)}, f32[24,1,130]{2,1,0:T(1,128)S(1)}, u32[]{:S(2)}, u32[]{:S(2)}) collective-permute-start(f32[24,1,130]{2,1,0:T(1,128)S(1)} %get-tuple-element.24), channel_id=1, source_target_pairs={{1,0},{2,1},{3,2},{4,3},{5,4},{6,5},{7,6},{8,7},{9,8},{10,9},{11,1... | collective-permute-start | bytes 37448 | tf_op jit(solution)/shard_map/ppermute | solution.py:19
  159.6 33.3 %copy-start.5 = (f32[12,96,128]{2,1,0:T(8,128)}, f32[12,96,128]{2,1,0:T(8,128)S(1)}, u32[]{:S(2)}) copy-start(f32[12,96,128]{2,1,0:T(8,128)S(1)} %get-tuple-element.45) | copy-start | bytes 1769476
  160.8 10.2 %collective-permute-start.8 = (f32[24,96,1]{1,0,2:T(8,128)S(1)}, f32[24,96,1]{1,0,2:T(8,128)S(1)}, u32[]{:S(2)}, u32[]{:S(2)}) collective-permute-start(f32[24,96,1]{1,0,2:T(8,128)S(1)} %copy.27), channel_id=1, source_target_pairs={{16,0},{32,16},{48,32},{64,48},{80,64},{96,80},{112,96},{128,112},... | collective-permute-start | bytes 27656 | tf_op jit(solution)/shard_map/ppermute | solution.py:19
  169.1 9.3 %collective-permute-start.9 = (f32[24,96,1]{1,0,2:T(8,128)S(1)}, f32[24,96,1]{1,0,2:T(8,128)}, u32[]{:S(2)}, u32[]{:S(2)}) collective-permute-start(f32[24,96,1]{1,0,2:T(8,128)S(1)} %copy.29), channel_id=1, source_target_pairs={{0,16},{16,32},{32,48},{48,64},{64,80},{80,96},{96,112},{112,128},... | collective-permute-start | bytes 27656 | tf_op jit(solution)/shard_map/ppermute | solution.py:18
  179.5 13.3 %copy-start.7 = (f32[12,96,128]{2,1,0:T(8,128)S(1)}, f32[12,96,128]{2,1,0:T(8,128)}, u32[]{:S(2)}) copy-start(f32[12,96,128]{2,1,0:T(8,128)} %copy-done.6) | copy-start | bytes 1769476
  179.5 13.3 %copy-start.34 = (f32[96]{0:T(128)S(1)}, f32[96]{0:T(128)}, u32[]{:S(2)}) copy-start(f32[96]{0:T(128)} %copy-done.33) | copy-start | bytes 1156
  180.7 6.9 %collective-permute-start.10 = (f32[24,1,130]{2,1,0:T(1,128)S(1)}, f32[24,1,130]{2,1,0:T(1,128)S(1)}, u32[]{:S(2)}, u32[]{:S(2)}) collective-permute-start(f32[24,1,130]{2,1,0:T(1,128)S(1)} %get-tuple-element.21), channel_id=1, source_target_pairs={{1,0},{2,1},{3,2},{4,3},{5,4},{6,5},{7,6},{8,7},{9,8},{10,9},{11,1... | collective-permute-start | bytes 37448 | tf_op jit(solution)/shard_map/ppermute | solution.py:19
  185.6 8.2 %copy-start.39 = (f32[6]{0:T(128)S(1)}, f32[6]{0:T(128)}, u32[]{:S(2)}) copy-start(f32[6]{0:T(128)} %constant.32) | copy-start | bytes 76
  185.6 7.3 %collective-permute-start.11 = (f32[24,1,130]{2,1,0:T(1,128)S(1)}, f32[24,1,130]{2,1,0:T(1,128)S(1)}, u32[]{:S(2)}, u32[]{:S(2)}) collective-permute-start(f32[24,1,130]{2,1,0:T(1,128)S(1)} %get-tuple-element.22), channel_id=1, source_target_pairs={{0,1},{1,2},{2,3},{3,4},{4,5},{5,6},{6,7},{7,8},{8,9},{9,10},{10,1... | collective-permute-start | bytes 37448 | tf_op jit(solution)/shard_map/ppermute | solution.py:18
  (21 other events, 24.0 us)
Sparse Core Ops, SparseCore 0:
  11.5 69.0 all-gather.1
where the time goes:
time: 203 us; the launch traced here: 202 us
  waiting for transfers between devices  89.7 us (44%)
  starting transfers between devices  51.2 us (25%)
  local copies, waits for them, and re-layouts  17.9 us (9%)
  other arithmetic  17.9 us (9%)
  between operations  14.7 us (7%)
  matrix products  10.9 us (5%)
    all_gather x1, waiting for transfers between devices, per_device(): lax.all_gather(mixed, 'lat', axis=1, tiled=True)  67.3 us
    ppermute x6, starting transfers between devices, extended(): after = lax.ppermute(initial, axis, down)  39.7 us
    ppermute x6, waiting for transfers between devices, extended(): before = lax.ppermute(last, axis, up)  18.6 us
    ppermute x6, starting transfers between devices, extended(): before = lax.ppermute(last, axis, up)  11.5 us
    dot_general x1, matrix products, per_device(): jnp.einsum('rs,ksc->krc', lat_green, lax.all_gather(mixed, 'lat', axis=1,...  8.35 us
  transfers between devices with their start and end apart: 13, of which 7 were waited for; matrix products, arithmetic and copies ran while one was open for 3% of the time, Pallas kernels for 0%

commit v1 on v0

--- a/solution.py
+++ b/solution.py
@@ -6,6 +6,19 @@
 
 FREQS = [1.9323, 2.0, 1.896, 2.0055, 1.0027, 0.9295]
 VISCOSITY = 0.5
+
+
+def enter_the_streams(z, axis_name):
+    a_now = jnp.concatenate(
+        jax.lax.all_to_all(
+            jnp.stack([z] * jax.lax.axis_size(axis_name)),
+            axis_name=axis_name,
+            split_axis=0,
+            concat_axis=0,
+        ),
+        1,
+    )
+    return a_now
 
 
 def extended(array, sides, width, wrap):
@@ -91,10 +104,7 @@
     source = wet_frac * elevation
     mixed = jnp.einsum("krj,cj->krc", source, lon_green, precision=lax.Precision.HIGHEST)
     sal = jnp.einsum(
-        "rs,ksc->krc",
-        lat_green,
-        lax.all_gather(mixed, "lat", axis=1, tiled=True),
-        precision=lax.Precision.HIGHEST,
+        "rs,ksc->krc", lat_green, enter_the_streams(mixed, "lat"), precision=lax.Precision.HIGHEST
     )
     potential = elevation - equilibrium - sal
     first_row = lax.axis_index("lat") * rows_here

time: 203 us -> 281 us (1.38)
  waiting for transfers between devices: 89.7 us -> 159 us
  starting transfers between devices: 51.2 us -> 67.4 us
  between operations: 14.7 us -> 1.31 us
  local copies, waits for them, and re-layouts: 17.9 us -> 27.4 us
  matrix products: 10.9 us -> 7.54 us
    all_to_all x0 -> x1, waiting for transfers between devices: none -> 136 us  [enter_the_streams(): jax.lax.all_to_all(jnp.stack([z] * jax.lax.axis_size(axis_name)), axis_na...]
    all_gather x1 -> x0, waiting for transfers between devices: 67.3 us -> none  [per_device(): lax.all_gather(mixed, 'lat', axis=1, tiled=True)]
    all_to_all x0 -> x1, starting transfers between devices: none -> 10.6 us  [enter_the_streams(): jax.lax.all_to_all(jnp.stack([z] * jax.lax.axis_size(axis_name)), axis_na...]
    ppermute x6, starting transfers between devices: 39.7 us -> 45.3 us  [extended(): after = lax.ppermute(initial, axis, down)]
    another operation x0 -> x1, local copies, waits for them, and re-layouts: none -> 4.79 us  [enter_the_streams(): jnp.stack([z] * jax.lax.axis_size(axis_name))]
    reshape x0 -> x1, local copies, waits for them, and re-layouts: none -> 4.62 us  [enter_the_streams(): jnp.concatenate(jax.lax.all_to_all(jnp.stack([z] * jax.lax.axis_size(axis...]
  transfers between devices with their start and end apart: 13 -> 13, of which waited for: 7 -> 7; matrix products, arithmetic and copies ran while one was open for 3% -> 2% of each run, Pallas kernels for 0% -> 0%
where the time goes in v1:
time: 281 us; the launch traced here: 280 us
  waiting for transfers between devices  159 us (57%)
  starting transfers between devices  67.4 us (24%)
  local copies, waits for them, and re-layouts  27.4 us (10%)
  other arithmetic  17.8 us (6%)
  matrix products  7.54 us (3%)
    all_to_all x1, waiting for transfers between devices, enter_the_streams(): jax.lax.all_to_all(jnp.stack([z] * jax.lax.axis_size(axis_name)), axis_na...  136 us
    ppermute x6, starting transfers between devices, extended(): after = lax.ppermute(initial, axis, down)  45.3 us
    ppermute x6, waiting for transfers between devices, extended(): before = lax.ppermute(last, axis, up)  18.6 us
    ppermute x6, starting transfers between devices, extended(): before = lax.ppermute(last, axis, up)  11.5 us
    all_to_all x1, starting transfers between devices, enter_the_streams(): jax.lax.all_to_all(jnp.stack([z] * jax.lax.axis_size(axis_name)), axis_na...  10.6 us
    dot_general x1, matrix products, per_device(): jnp.einsum('rs,ksc->krc', lat_green, enter_the_streams(mixed, 'lat'), pre...  5.84 us
  transfers between devices with their start and end apart: 13, of which 7 were waited for; matrix products, arithmetic and copies ran while one was open for 2% of the time, Pallas kernels for 0%

profile of v1, /device:TPU:2, one launch (start us, length us, event | category | flops | bytes accessed | tf_op | source)
XLA Modules:
  0.0 280.1 jit_solution(6858664172806704771)
XLA Ops:
  2.1 1.7 fusion.20
  3.8 4.8 %stack.2 = f32[16,12,96,128]{3,2,1,0:T(8,128)} broadcast(f32[12,96,128]{2,1,0:T(8,128)S(1)} %fusion.20), dimensions={1,2,3} | broadcast | bytes 10027008 | tf_op jit(solution)/shard_map/stack | solution.py:14
  8.6 10.6 %all-to-all-start = ((f32[16,12,96,128]{3,2,1,0:T(8,128)}), f32[16,12,96,128]{3,2,1,0:T(8,128)}, u32[]{:S(2)}, u32[]{:S(2)}) async-start(f32[16,12,96,128]{3,2,1,0:T(8,128)} %stack.2), calls=%async_computation | async-start | bytes 18874368 | tf_op jit(solution)/shard_map/all_to_all | solution.py:13
  21.2 136.3 %all-to-all-done = f32[16,12,96,128]{3,2,1,0:T(8,128)} async-done(((f32[16,12,96,128]{3,2,1,0:T(8,128)}), f32[16,12,96,128]{3,2,1,0:T(8,128)}, u32[]{:S(2)}, u32[]{:S(2)}) %all-to-all-start) | async-done | bytes 9437216 | tf_op jit(solution)/shard_map/all_to_all | solution.py:13
  157.5 4.6 %copy.15 = f32[12,16,96,128]{3,2,1,0:T(8,128)S(1)} copy(f32[12,16,96,128]{3,2,0,1:T(8,128)} %bitcast.1) | data formatting | bytes 18874368 | tf_op jit(solution)/shard_map/reshape | solution.py:12
  162.1 5.8 %fusion = f32[12,96,128]{2,1,0:T(8,128)S(1)} fusion(f32[12,1536,128]{2,1,0:T(8,128)S(1)} %bitcast.13, f32[96,1536]{1,0:T(8,128)S(1)} %copy-done, f32[12,96,128]{2,1,0:T(8,128)S(1)} %copy-done.11, f32[12,96,128]{2,1,0:T(8,128)S(1)} %copy-done.21), kind=kOutput, calls=%fused_computation.11 | convolution fusion | flops 2718203904 | bytes 11796480 | tf_op jit(solution)/shard_map/rs,ksc->krc/dot_general | solution.py:106
  168.1 1.9 fusion.56
  170.0 2.6 copy.16
  172.6 8.4 %collective-permute-start = (f32[36,96,1]{1,2,0:T(1,128)}, f32[36,96,1]{1,2,0:T(1,128)}, u32[]{:S(2)}, u32[]{:S(2)}) collective-permute-start(f32[36,96,1]{1,2,0:T(1,128)} %copy.16), channel_id=1, source_target_pairs={{16,0},{32,16},{48,32},{64,48},{80,64},{96,80},{112,96},{128,112},... | collective-permute-start | bytes 41480 | tf_op jit(solution)/shard_map/ppermute | solution.py:32
  182.2 1.9 collective-permute-start.1
  184.2 1.3 copy.17
  185.5 6.3 %collective-permute-done.1 = f32[36,96,1]{1,2,0:T(1,128)} collective-permute-done((f32[36,96,1]{1,2,0:T(1,128)}, f32[36,96,1]{1,2,0:T(1,128)}, u32[]{:S(2)}, u32[]{:S(2)}) %collective-permute-start.1) | collective-permute-done | bytes 13856 | tf_op jit(solution)/shard_map/ppermute | solution.py:31
  191.8 2.5 copy.19
  194.3 1.4 pad_maximum_fusion.47
  195.7 1.9 collective-permute-start.2
  197.7 10.6 %collective-permute-start.3 = (f32[36,1,130]{2,1,0:T(1,128)S(1)}, f32[36,1,130]{2,1,0:T(1,128)S(1)}, u32[]{:S(2)}, u32[]{:S(2)}) collective-permute-start(f32[36,1,130]{2,1,0:T(1,128)S(1)} %get-tuple-element.20), channel_id=1, source_target_pairs={{1,0},{2,1},{3,2},{4,3},{5,4},{6,5},{7,6},{8,7},{9,8},{10,9},{11,1... | collective-permute-start | bytes 56168 | tf_op jit(solution)/shard_map/ppermute | solution.py:32
  208.4 1.4 collective-permute-done.3
  209.7 2.3 fusion.4
  212.1 1.4 fusion.16
  213.5 1.3 fusion.13
  217.5 1.9 collective-permute-start.4
  219.8 7.5 %collective-permute-start.5 = (f32[24,96,1]{1,0,2:T(8,128)S(1)}, f32[24,96,1]{1,0,2:T(8,128)}, u32[]{:S(2)}, u32[]{:S(2)}) collective-permute-start(f32[24,96,1]{1,0,2:T(8,128)S(1)} %copy.23), channel_id=1, source_target_pairs={{16,0},{32,16},{48,32},{64,48},{80,64},{96,80},{112,96},{128,112},... | collective-permute-start | bytes 27656 | tf_op jit(solution)/shard_map/ppermute | solution.py:32
  231.0 1.9 collective-permute-start.6
  232.9 5.9 %collective-permute-start.7 = (f32[24,1,130]{2,1,0:T(1,128)S(1)}, f32[24,1,130]{2,1,0:T(1,128)S(1)}, u32[]{:S(2)}, u32[]{:S(2)}) collective-permute-start(f32[24,1,130]{2,1,0:T(1,128)S(1)} %get-tuple-element.24), channel_id=1, source_target_pairs={{1,0},{2,1},{3,2},{4,3},{5,4},{6,5},{7,6},{8,7},{9,8},{10,9},{11,1... | collective-permute-start | bytes 37448 | tf_op jit(solution)/shard_map/ppermute | solution.py:32
  238.8 1.5 collective-permute-done.7
  240.3 1.6 fusion.1
  245.5 7.9 %collective-permute-start.8 = (f32[24,96,1]{1,0,2:T(8,128)S(1)}, f32[24,96,1]{1,0,2:T(8,128)S(1)}, u32[]{:S(2)}, u32[]{:S(2)}) collective-permute-start(f32[24,96,1]{1,0,2:T(8,128)S(1)} %copy.28), channel_id=1, source_target_pairs={{16,0},{32,16},{48,32},{64,48},{80,64},{96,80},{112,96},{128,112},... | collective-permute-start | bytes 27656 | tf_op jit(solution)/shard_map/ppermute | solution.py:32
  253.8 1.9 collective-permute-start.9
  256.2 6.9 %collective-permute-done.9 = f32[24,96,1]{1,0,2:T(8,128)} collective-permute-done((f32[24,96,1]{1,0,2:T(8,128)S(1)}, f32[24,96,1]{1,0,2:T(8,128)}, u32[]{:S(2)}, u32[]{:S(2)}) %collective-permute-start.9) | collective-permute-done | bytes 9248 | tf_op jit(solution)/shard_map/ppermute | solution.py:31
  265.4 4.9 %collective-permute-start.10 = (f32[24,1,130]{2,1,0:T(1,128)S(1)}, f32[24,1,130]{2,1,0:T(1,128)S(1)}, u32[]{:S(2)}, u32[]{:S(2)}) collective-permute-start(f32[24,1,130]{2,1,0:T(1,128)S(1)} %get-tuple-element.21), channel_id=1, source_target_pairs={{1,0},{2,1},{3,2},{4,3},{5,4},{6,5},{7,6},{8,7},{9,8},{10,9},{11,1... | collective-permute-start | bytes 37448 | tf_op jit(solution)/shard_map/ppermute | solution.py:32
  270.3 1.9 collective-permute-start.11
  272.2 5.3 %collective-permute-done.11 = f32[24,1,130]{2,1,0:T(1,128)S(1)} collective-permute-done((f32[24,1,130]{2,1,0:T(1,128)S(1)}, f32[24,1,130]{2,1,0:T(1,128)S(1)}, u32[]{:S(2)}, u32[]{:S(2)}) %collective-permute-start.11) | collective-permute-done | bytes 12512 | tf_op jit(solution)/shard_map/ppermute | solution.py:31
  (117 shorter events, 20.3 us)
Async XLA Ops:
  0.6 161.5 %copy-start = (f32[96,1536]{1,0:T(8,128)S(1)}, f32[96,1536]{1,0:T(8,128)}, u32[]{:S(2)}) copy-start(f32[96,1536]{1,0:T(8,128)} %param.20) | copy-start | bytes 1769476
  8.6 11.2 %copy-start.26 = (f32[96,128]{1,0:T(8,128)S(1)}, f32[96,128]{1,0:T(8,128)}, u32[]{:S(2)}) copy-start(f32[96,128]{1,0:T(8,128)} %param.16) | copy-start | bytes 147460
  8.6 11.9 %copy-start.27 = (f32[96,128]{1,0:T(8,128)S(1)}, f32[96,128]{1,0:T(8,128)}, u32[]{:S(2)}) copy-start(f32[96,128]{1,0:T(8,128)} %param.17) | copy-start | bytes 147460
  8.6 148.8 %all-to-all-start = ((f32[16,12,96,128]{3,2,1,0:T(8,128)}), f32[16,12,96,128]{3,2,1,0:T(8,128)}, u32[]{:S(2)}, u32[]{:S(2)}) async-start(f32[16,12,96,128]{3,2,1,0:T(8,128)} %stack.2), calls=%async_computation | async-start | bytes 18874368 | tf_op jit(solution)/shard_map/all_to_all | solution.py:13
  19.8 195.0 %copy-start.35 = (f32[96]{0:T(128)}, f32[96]{0:T(128)S(1)}, u32[]{:S(2)}) copy-start(f32[96]{0:T(128)S(1)} %get-tuple-element.54) | copy-start | bytes 1156
  157.5 4.6 %copy-start.11 = (f32[12,96,128]{2,1,0:T(8,128)S(1)}, f32[12,96,128]{2,1,0:T(8,128)}, u32[]{:S(2)}) copy-start(f32[12,96,128]{2,1,0:T(8,128)} %param.12) | copy-start | bytes 1769476
  157.5 4.7 %copy-start.21 = (f32[12,96,128]{2,1,0:T(8,128)S(1)}, f32[12,96,128]{2,1,0:T(8,128)}, u32[]{:S(2)}) copy-start(f32[12,96,128]{2,1,0:T(8,128)} %param.13) | copy-start | bytes 1769476
  162.1 5.9 %copy-start.2 = (f32[12,96,128]{2,1,0:T(8,128)S(1)}, f32[12,96,128]{2,1,0:T(8,128)}, u32[]{:S(2)}) copy-start(f32[12,96,128]{2,1,0:T(8,128)} %param.15) | copy-start | bytes 1769476
  162.1 5.9 %copy-start.3 = (f32[12,96,128]{2,1,0:T(8,128)S(1)}, f32[12,96,128]{2,1,0:T(8,128)}, u32[]{:S(2)}) copy-start(f32[12,96,128]{2,1,0:T(8,128)} %param.14) | copy-start | bytes 1769476
  172.6 11.5 %collective-permute-start = (f32[36,96,1]{1,2,0:T(1,128)}, f32[36,96,1]{1,2,0:T(1,128)}, u32[]{:S(2)}, u32[]{:S(2)}) collective-permute-start(f32[36,96,1]{1,2,0:T(1,128)} %copy.16), channel_id=1, source_target_pairs={{16,0},{32,16},{48,32},{64,48},{80,64},{96,80},{112,96},{128,112},... | collective-permute-start | bytes 41480 | tf_op jit(solution)/shard_map/ppermute | solution.py:32
  182.2 9.6 %collective-permute-start.1 = (f32[36,96,1]{1,2,0:T(1,128)}, f32[36,96,1]{1,2,0:T(1,128)}, u32[]{:S(2)}, u32[]{:S(2)}) collective-permute-start(f32[36,96,1]{1,2,0:T(1,128)} %copy.18), channel_id=1, source_target_pairs={{0,16},{16,32},{32,48},{48,64},{64,80},{80,96},{96,112},{112,128},... | collective-permute-start | bytes 41480 | tf_op jit(solution)/shard_map/ppermute | solution.py:31
  184.2 27.9 %copy-start.33 = (f32[96]{0:T(128)}, f32[96]{0:T(128)S(1)}, u32[]{:S(2)}) copy-start(f32[96]{0:T(128)S(1)} %divide_multiply_fusion) | copy-start | bytes 1156
  194.3 15.4 %copy-start.1 = (f32[36,96,1]{2,1,0:T(8,128)S(1)}, f32[36,96,1]{2,1,0:T(8,128)}, u32[]{:S(2)}) copy-start(f32[36,96,1]{2,1,0:T(8,128)} %copy.19) | copy-start | bytes 41476
  194.3 15.4 %copy-start.4 = (f32[12,96,128]{2,1,0:T(8,128)S(1)}, f32[12,96,128]{2,1,0:T(8,128)}, u32[]{:S(2)}) copy-start(f32[12,96,128]{2,1,0:T(8,128)} %param.14) | copy-start | bytes 1769476
  195.7 12.6 %collective-permute-start.2 = (f32[36,1,130]{2,1,0:T(1,128)S(1)}, f32[36,1,130]{2,1,0:T(1,128)S(1)}, u32[]{:S(2)}, u32[]{:S(2)}) collective-permute-start(f32[36,1,130]{2,1,0:T(1,128)S(1)} %get-tuple-element.19), channel_id=1, source_target_pairs={{0,1},{1,2},{2,3},{3,4},{4,5},{5,6},{6,7},{7,8},{8,9},{9,10},{10,1... | collective-permute-start | bytes 56168 | tf_op jit(solution)/shard_map/ppermute | solution.py:31
  197.7 12.1 %collective-permute-start.3 = (f32[36,1,130]{2,1,0:T(1,128)S(1)}, f32[36,1,130]{2,1,0:T(1,128)S(1)}, u32[]{:S(2)}, u32[]{:S(2)}) collective-permute-start(f32[36,1,130]{2,1,0:T(1,128)S(1)} %get-tuple-element.20), channel_id=1, source_target_pairs={{1,0},{2,1},{3,2},{4,3},{5,4},{6,5},{7,6},{8,7},{9,8},{10,9},{11,1... | collective-permute-start | bytes 56168 | tf_op jit(solution)/shard_map/ppermute | solution.py:32
  208.3 7.1 %copy-start.31 = (f32[96]{0:T(128)}, f32[96]{0:T(128)S(1)}, u32[]{:S(2)}) copy-start(f32[96]{0:T(128)S(1)} %fusion.52) | copy-start | bytes 1156
  217.5 9.9 %collective-permute-start.4 = (f32[24,96,1]{1,0,2:T(8,128)S(1)}, f32[24,96,1]{1,0,2:T(8,128)S(1)}, u32[]{:S(2)}, u32[]{:S(2)}) collective-permute-start(f32[24,96,1]{1,0,2:T(8,128)S(1)} %copy.22), channel_id=1, source_target_pairs={{0,16},{16,32},{32,48},{48,64},{64,80},{80,96},{96,112},{112,128},... | collective-permute-start | bytes 27656 | tf_op jit(solution)/shard_map/ppermute | solution.py:31
  219.8 8.9 %collective-permute-start.5 = (f32[24,96,1]{1,0,2:T(8,128)S(1)}, f32[24,96,1]{1,0,2:T(8,128)}, u32[]{:S(2)}, u32[]{:S(2)}) collective-permute-start(f32[24,96,1]{1,0,2:T(8,128)S(1)} %copy.23), channel_id=1, source_target_pairs={{16,0},{32,16},{48,32},{64,48},{80,64},{96,80},{112,96},{128,112},... | collective-permute-start | bytes 27656 | tf_op jit(solution)/shard_map/ppermute | solution.py:32
  229.9 10.5 %copy-start.9 = (f32[12,96,128]{2,1,0:T(8,128)S(1)}, f32[12,96,128]{2,1,0:T(8,128)}, u32[]{:S(2)}) copy-start(f32[12,96,128]{2,1,0:T(8,128)} %copy-done.8) | copy-start | bytes 1769476
  231.0 7.8 %collective-permute-start.6 = (f32[24,1,130]{2,1,0:T(1,128)S(1)}, f32[24,1,130]{2,1,0:T(1,128)S(1)}, u32[]{:S(2)}, u32[]{:S(2)}) collective-permute-start(f32[24,1,130]{2,1,0:T(1,128)S(1)} %get-tuple-element.23), channel_id=1, source_target_pairs={{0,1},{1,2},{2,3},{3,4},{4,5},{5,6},{6,7},{7,8},{8,9},{9,10},{10,1... | collective-permute-start | bytes 37448 | tf_op jit(solution)/shard_map/ppermute | solution.py:31
  232.9 9.1 %copy-start.10 = (f32[12,96,128]{2,1,0:T(8,128)S(1)}, f32[12,96,128]{2,1,0:T(8,128)}, u32[]{:S(2)}) copy-start(f32[12,96,128]{2,1,0:T(8,128)} %get-tuple-element.16) | copy-start | bytes 1769476
  232.9 9.1 %copy-start.12 = (f32[12,96,128]{2,1,0:T(8,128)S(1)}, f32[12,96,128]{2,1,0:T(8,128)}, u32[]{:S(2)}) copy-start(f32[12,96,128]{2,1,0:T(8,128)} %get-tuple-element.18) | copy-start | bytes 1769476
  232.9 7.4 %collective-permute-start.7 = (f32[24,1,130]{2,1,0:T(1,128)S(1)}, f32[24,1,130]{2,1,0:T(1,128)S(1)}, u32[]{:S(2)}, u32[]{:S(2)}) collective-permute-start(f32[24,1,130]{2,1,0:T(1,128)S(1)} %get-tuple-element.24), channel_id=1, source_target_pairs={{1,0},{2,1},{3,2},{4,3},{5,4},{6,5},{7,6},{8,7},{9,8},{10,9},{11,1... | collective-permute-start | bytes 37448 | tf_op jit(solution)/shard_map/ppermute | solution.py:32
  244.3 33.3 %copy-start.5 = (f32[12,96,128]{2,1,0:T(8,128)}, f32[12,96,128]{2,1,0:T(8,128)S(1)}, u32[]{:S(2)}) copy-start(f32[12,96,128]{2,1,0:T(8,128)S(1)} %get-tuple-element.45) | copy-start | bytes 1769476
  245.5 10.2 %collective-permute-start.8 = (f32[24,96,1]{1,0,2:T(8,128)S(1)}, f32[24,96,1]{1,0,2:T(8,128)S(1)}, u32[]{:S(2)}, u32[]{:S(2)}) collective-permute-start(f32[24,96,1]{1,0,2:T(8,128)S(1)} %copy.28), channel_id=1, source_target_pairs={{16,0},{32,16},{48,32},{64,48},{80,64},{96,80},{112,96},{128,112},... | collective-permute-start | bytes 27656 | tf_op jit(solution)/shard_map/ppermute | solution.py:32
  253.8 9.3 %collective-permute-start.9 = (f32[24,96,1]{1,0,2:T(8,128)S(1)}, f32[24,96,1]{1,0,2:T(8,128)}, u32[]{:S(2)}, u32[]{:S(2)}) collective-permute-start(f32[24,96,1]{1,0,2:T(8,128)S(1)} %copy.30), channel_id=1, source_target_pairs={{0,16},{16,32},{32,48},{48,64},{64,80},{80,96},{96,112},{112,128},... | collective-permute-start | bytes 27656 | tf_op jit(solution)/shard_map/ppermute | solution.py:31
  264.2 13.3 %copy-start.7 = (f32[12,96,128]{2,1,0:T(8,128)S(1)}, f32[12,96,128]{2,1,0:T(8,128)}, u32[]{:S(2)}) copy-start(f32[12,96,128]{2,1,0:T(8,128)} %copy-done.6) | copy-start | bytes 1769476
  264.2 13.3 %copy-start.34 = (f32[96]{0:T(128)S(1)}, f32[96]{0:T(128)}, u32[]{:S(2)}) copy-start(f32[96]{0:T(128)} %copy-done.33) | copy-start | bytes 1156
  265.4 6.9 %collective-permute-start.10 = (f32[24,1,130]{2,1,0:T(1,128)S(1)}, f32[24,1,130]{2,1,0:T(1,128)S(1)}, u32[]{:S(2)}, u32[]{:S(2)}) collective-permute-start(f32[24,1,130]{2,1,0:T(1,128)S(1)} %get-tuple-element.21), channel_id=1, source_target_pairs={{1,0},{2,1},{3,2},{4,3},{5,4},{6,5},{7,6},{8,7},{9,8},{10,9},{11,1... | collective-permute-start | bytes 37448 | tf_op jit(solution)/shard_map/ppermute | solution.py:32
  270.3 8.2 %copy-start.39 = (f32[6]{0:T(128)S(1)}, f32[6]{0:T(128)}, u32[]{:S(2)}) copy-start(f32[6]{0:T(128)} %constant.32) | copy-start | bytes 76
  270.3 7.3 %collective-permute-start.11 = (f32[24,1,130]{2,1,0:T(1,128)S(1)}, f32[24,1,130]{2,1,0:T(1,128)S(1)}, u32[]{:S(2)}, u32[]{:S(2)}) collective-permute-start(f32[24,1,130]{2,1,0:T(1,128)S(1)} %get-tuple-element.22), channel_id=1, source_target_pairs={{0,1},{1,2},{2,3},{3,4},{4,5},{5,6},{6,7},{7,8},{8,9},{9,10},{10,1... | collective-permute-start | bytes 37448 | tf_op jit(solution)/shard_map/ppermute | solution.py:31
  (21 other events, 23.8 us)
